TPU v7x, 512 devices: a whole 4x4x16 slice. The times are simulated.
512 devices in a mesh: pool: 128 (over x, z, core), tp: 4 (over y).
Axes of the slice: x: 4, y: 4, z: 16, core: 2. Of those that a mesh axis runs over, the one named last changes fastest.
Arguments:
- hidden_rows: bfloat16 [16384, 8192], P('pool', 'tp'), may hold values from -6 to 6
- kv_weight: bfloat16 [8192, 1024], P('tp', 'pool'), may hold values from -0.0625 to 0.0625
- queries: bfloat16 [16384, 4096], P('pool', 'tp'), may hold values from -5 to 5
- cache_table: bfloat16 [1024, 128, 1024], P('pool', None, 'tp'), may hold values from -5 to 5
- retrieval: int32 [128, 64], P('pool'), may hold values from 0 to 1023, as said below
- pattern: int32 [128, 2, 64], P('pool'), may hold values 0 or 1
Outputs:
- attended: bfloat16 [16384, 4096], P('pool', 'tp')
- fresh_kv: bfloat16 [16384, 1024], P('pool', 'tp')
Inputs may be any that keep to these rules, and one draw needn't show every extreme that they name: `retrieval`: each request names 64 blocks held by 64 different devices (block b is held by device b // 8); one device, drawn from the seed, holds a block named by every request.
All inputs are finite; a program needn't handle non-finite values. No bound on the sum of `pattern` on one device may be relied on, other than what follows from the above.
Results may differ from a plain program's by a relative error of at most 0.025.
Values may be sent and summed in bfloat16 or wider, within the bound.
No kernel may reach another device: no remote copies, remote signals or barrier semaphores. Data moves between devices by JAX's collectives and lax.ppermute only.
A program may use at most 192 MiB of HBM per device.

v0:
```python
import math
import jax
import jax.numpy as jnp
from jax import lax
from jax.sharding import PartitionSpec as P

HD = 128
QH = 32
KVH = 4
BLK = 128
RBLK = 64


def rows_by_keys(left, right):
    return lax.dot_general(
        left, right, (((1,), (1,)), ((), ())), preferred_element_type=jnp.float32
    )


def body(hidden_rows, kv_weight, queries, cache_table, retrieval, pattern):
    partial_kv = jnp.dot(
        hidden_rows,
        lax.all_gather(kv_weight, "pool", axis=1, tiled=True),
        preferred_element_type=jnp.float32,
    )
    fresh = lax.psum_scatter(partial_kv.astype(jnp.bfloat16), "tp", scatter_dimension=1, tiled=True)
    wanted = retrieval[0]
    blocks_dev = cache_table.shape[0]
    npool = lax.axis_size("pool")
    owners = wanted // blocks_dev
    local = wanted % blocks_dev
    hits = (owners[:, None] == jnp.arange(npool, dtype=jnp.int32)[None, :]).astype(jnp.int32)
    request = jnp.sum(hits * (local + 1)[:, None], axis=0)
    incoming = lax.all_to_all(
        request.reshape(npool, 1), "pool", split_axis=0, concat_axis=0, tiled=True
    ).reshape(npool)
    reply = jnp.zeros((npool,) + cache_table.shape[1:], jnp.bfloat16)
    for slot in range(blocks_dev):
        reply = jnp.where((incoming == slot + 1)[:, None, None], cache_table[slot][None], reply)
    arrived = lax.all_to_all(reply, "pool", split_axis=0, concat_axis=0, tiled=True)
    fetched = jnp.take(arrived, owners, axis=0)
    count = hidden_rows.shape[0]
    fetch_count = wanted.shape[0]
    group = QH // KVH
    scale = float(HD) ** (-0.5)
    local_heads = fresh.shape[1] // (2 * HD)
    width = fetched.shape[2]
    per_step = math.gcd(fetch_count, 8)
    steps_count = fetch_count // per_step
    grouped = fetched.reshape(steps_count, per_step * BLK, width)
    pat_steps = jnp.transpose(
        pattern[0].reshape(pattern.shape[1], steps_count, per_step), (1, 0, 2)
    )
    token_of_row = jnp.arange(count * group) // group
    block_of_row = token_of_row // RBLK
    row_blocks = block_of_row[:, None, None] == jnp.arange(pattern.shape[1])[None, :, None]
    near_mask = token_of_row[:, None] >= jnp.arange(count)[None, :]
    q_heads = queries.reshape(count, local_heads, group * HD)
    q_rows = q_heads[:, 0].reshape(count * group, HD)
    near_keys = fresh[:, 0:HD]
    near_vals = fresh[:, HD : 2 * HD]
    near_scores = rows_by_keys(q_rows, near_keys) * scale
    top = jnp.max(jnp.where(near_mask, near_scores, -1e30), axis=1)
    weights = jnp.where(near_mask, jnp.exp(near_scores - top[:, None]), 0.0)
    total = jnp.sum(weights, axis=1)
    numer = jnp.dot(weights.astype(jnp.bfloat16), near_vals, preferred_element_type=jnp.float32)

    def visit(carry, items):
        top_now, total_now, numer_now = carry
        block_rows, pat_now = items
        keys = block_rows[:, 0:HD]
        vals = block_rows[:, HD : 2 * HD]
        scores = rows_by_keys(q_rows, keys) * scale
        row_pat = jnp.any(row_blocks & (pat_now[None] != 0), axis=1)
        mask = jnp.repeat(row_pat, BLK, axis=1)
        top_new = jnp.maximum(top_now, jnp.max(jnp.where(mask, scores, -1e30), axis=1))
        weights_now = jnp.where(mask, jnp.exp(scores - top_new[:, None]), 0.0)
        factor = jnp.exp(top_now - top_new)
        total_new = total_now * factor + jnp.sum(weights_now, axis=1)
        numer_new = numer_now * factor[:, None] + jnp.dot(
            weights_now.astype(jnp.bfloat16), vals, preferred_element_type=jnp.float32
        )
        return ((top_new, total_new, numer_new), None)

    (top, total, numer), unused = lax.scan(visit, (top, total, numer), (grouped, pat_steps))
    results = (numer / total[:, None]).reshape(count, group * HD)
    attended = results.astype(jnp.bfloat16)
    return (attended, fresh)


def solution(mesh):
    placed = (
        P("pool", "tp"),
        P("tp", "pool"),
        P("pool", "tp"),
        P("pool", None, "tp"),
        P("pool", None),
        P("pool", None, None),
    )
    return jax.shard_map(
        body,
        mesh=mesh,
        in_specs=placed,
        out_specs=(P("pool", "tp"), P("pool", "tp")),
        check_vma=False,
    )
```

profile of v0, /device:TPU:24, one launch (start us, length us, event | category | flops | bytes accessed | tf_op | source)
XLA Modules:
  0.0 508.4 jit_solution(17769728993314333137)
XLA Ops:
  8.8 19.8 %all-to-all-start = ((s32[128,1,1]{2,1,0:T(1,128)}), s32[128,1,1]{2,1,0:T(1,128)S(1)}, u32[]{:S(2)}, u32[]{:S(2)}) async-start(s32[128,1,1]{2,1,0:T(1,128)} %copy.22), calls=%async_computation.1 | async-start | bytes 131072 | tf_op jit(solution)/shard_map/all_to_all | solution.py:34
  28.5 1.1 slice_bitcast_fusion.7
  29.6 14.4 %all-to-all-done = s32[128,1,1]{2,1,0:T(1,128)S(1)} async-done(((s32[128,1,1]{2,1,0:T(1,128)}), s32[128,1,1]{2,1,0:T(1,128)S(1)}, u32[]{:S(2)}, u32[]{:S(2)}) %all-to-all-start) | async-done | bytes 544 | tf_op jit(solution)/shard_map/all_to_all | solution.py:34
  44.0 18.3 %compare_reduce_fusion.7 = (pred[128]{0:T(512)(128)(4,1)S(1)}, pred[128]{0:T(512)(128)(4,1)S(1)}, pred[128]{0:T(512)(128)(4,1)S(1)}, pred[128]{0:T(512)(128)(4,1...) fusion(s32[128,1,1]{2,1,0:T(1,128)S(1)} %all-to-all-done), kind=kLoop, calls=%fused_computation.42 | loop fusion | flops 1024 | bytes 1536 | tf_op jit(solution)/shard_map/eq | solution.py:39
  62.4 7.7 %select_select_fusion = bf16[128,128,256]{2,1,0:T(8,128)(2,1)} fusion(pred[128]{0:T(512)(128)(4,1)S(1)} %get-tuple-element.107, pred[128]{0:T(512)(128)(4,1)S(1)} %get-tuple-element.108, pred[128]{0:T(512)(128)(4,1)S(1)} %get-tuple-element.109, pred[128]{0:T(512)(128)(4,1)S(1)} %get-tuple-element.110, pred[128]{0:T(512)(128)(4,1)S(1)} %get-tuple-element.111, ...), kind=kLoop, calls=%fused_computation.20 | loop fusion | flops 33554432 | bytes 8913920 | tf_op jit(solution)/shard_map/jit(_where)/select_n | solution.py:39
  70.1 7.6 %all-to-all-start.1 = ((bf16[128,128,256]{2,1,0:T(8,128)(2,1)}), bf16[128,128,256]{2,1,0:T(8,128)(2,1)}, u32[]{:S(2)}, u32[]{:S(2)}) async-start(bf16[128,128,256]{2,1,0:T(8,128)(2,1)} %select_select_fusion), calls=%async_computation.2 | async-start | bytes 16777216 | tf_op jit(solution)/shard_map/all_to_all | solution.py:40
  80.1 198.2 %all-gather.2.cloned.1.call-done = bf16[2048,1024]{0,1:T(8,128)(2,1)} async-done(((bf16[2048,8]{0,1:T(8,128)(2,1)}), bf16[2048,1024]{0,1:T(8,128)(2,1)}) %all-gather.2.cloned.1.call-update) | async-done | bytes 4194320 | tf_op jit(solution)/shard_map/all_gather | solution.py:23
  278.3 4.4 convolution_convert_fusion
  282.8 28.2 %reduce-scatter.2.cloned.1.call-done = bf16[128,256]{1,0:T(8,128)(2,1)} async-done(((bf16[128,1024]{1,0:T(8,128)(2,1)}), bf16[128,256]{1,0:T(8,128)(2,1)}) %reduce-scatter.2.cloned.1.call-update) | async-done | bytes 65552 | tf_op jit(solution)/shard_map/reduce_scatter | solution.py:26
  311.1 1.0 select_reduce_fusion
  312.2 1.0 fusion.12
  313.2 144.4 %all-to-all-done.1 = bf16[128,128,256]{2,1,0:T(8,128)(2,1)} async-done(((bf16[128,128,256]{2,1,0:T(8,128)(2,1)}), bf16[128,128,256]{2,1,0:T(8,128)(2,1)}, u32[]{:S(2)}, u32[]{:S(2)}) %all-to-all-start.1) | async-done | bytes 8388640 | tf_op jit(solution)/shard_map/all_to_all | solution.py:40
  457.7 6.2 %gather_fusion = bf16[64,128,256]{2,1,0:T(8,128)(2,1)} fusion(bf16[128,128,256]{2,1,0:T(8,128)(2,1)} %all-to-all-done.1, s32[1024]{0:T(1024)S(1)} %pad_clamp_fusion), kind=kCustom, calls=%fused_computation | custom fusion | bytes 8388864 | tf_op jit(solution)/shard_map/jit(_take)/gather | solution.py:41
  463.8 5.3 %bitcast_select_fusion.2 = bf16[8,1024,256]{2,1,0:T(8,128)(2,1)} fusion(pred[8,1024]{1,0:T(8,128)(4,1)S(1)} %broadcast_bitcast_fusion, bf16[8,1024,256]{2,1,0:T(8,128)(2,1)} %bitcast.104), kind=kLoop, calls=%fused_computation.21 | loop fusion | flops 2097152 | bytes 8396800 | tf_op jit(solution)/shard_map/jit(_take)/select_n | solution.py:41
  469.1 31.4 %while.15 = (s32[]{:T(128)}, f32[1024]{0:T(1024)S(1)}, f32[1024]{0:T(1024)S(1)}, f32[1024,128]{1,0:T(8,128)S(1)}, s32[8,2,8]{2,0,1:T(8,128)S(1)}, /*index=5*/bf1...) while((s32[]{:T(128)}, f32[1024]{0:T(1024)S(1)}, ...), condition=%wide.region_8.9_spmd.clone, body=%wide.region_4.8_spmd.clone.sunk | while | flops 545550336 | bytes 15561029 | solution.py:85
  469.2 1.1 dynamic-slice_bitcast_fusion.2
  472.0 1.0 convolution_add_fusion.2
  473.2 1.1 dynamic-slice_bitcast_fusion.2
  477.1 1.1 dynamic-slice_bitcast_fusion.2
  481.0 1.1 dynamic-slice_bitcast_fusion.2
  485.0 1.1 dynamic-slice_bitcast_fusion.2
  488.9 1.1 dynamic-slice_bitcast_fusion.2
  492.8 1.1 dynamic-slice_bitcast_fusion.2
  496.7 1.1 dynamic-slice_bitcast_fusion.2
  (109 shorter events, 26.4 us)
Async XLA Ops:
  7.2 271.1 %copy-start = (bf16[128,2048]{1,0:T(8,128)(2,1)S(1)}, bf16[128,2048]{1,0:T(8,128)(2,1)}, u32[]{:S(2)}) copy-start(bf16[128,2048]{1,0:T(8,128)(2,1)} %param.8) | copy-start | bytes 1572868
  8.8 35.3 %all-to-all-start = ((s32[128,1,1]{2,1,0:T(1,128)}), s32[128,1,1]{2,1,0:T(1,128)S(1)}, u32[]{:S(2)}, u32[]{:S(2)}) async-start(s32[128,1,1]{2,1,0:T(1,128)} %copy.22), calls=%async_computation.1 | async-start | bytes 131072 | tf_op jit(solution)/shard_map/all_to_all | solution.py:34
  70.1 8.9 %copy-start.3 = (s32[1,64]{1,0:T(1,128)S(1)}, s32[1,64]{1,0:T(1,128)}, u32[]{:S(2)}) copy-start(s32[1,64]{1,0:T(1,128)} %param.12) | copy-start | bytes 772
  70.1 9.8 %copy-start.1 = (bf16[128,1024]{1,0:T(8,128)(2,1)S(1)}, bf16[128,1024]{1,0:T(8,128)(2,1)}, u32[]{:S(2)}) copy-start(bf16[128,1024]{1,0:T(8,128)(2,1)} %param.10) | copy-start | bytes 786436
  70.1 9.9 %copy-start.2 = (s32[1,2,64]{2,1,0:T(2,128)S(1)}, s32[1,2,64]{2,1,0:T(2,128)}, u32[]{:S(2)}) copy-start(s32[1,2,64]{2,1,0:T(2,128)} %param.13) | copy-start | bytes 1540
  70.1 387.6 %all-to-all-start.1 = ((bf16[128,128,256]{2,1,0:T(8,128)(2,1)}), bf16[128,128,256]{2,1,0:T(8,128)(2,1)}, u32[]{:S(2)}, u32[]{:S(2)}) async-start(bf16[128,128,256]{2,1,0:T(8,128)(2,1)} %select_select_fusion), calls=%async_computation.2 | async-start | bytes 16777216 | tf_op jit(solution)/shard_map/all_to_all | solution.py:40
  77.7 200.6 %all-gather.2.cloned.1.call-start = ((), (), s32[]{:S(2)}) async-start(), calls=%async_computation.3 | async-start | bytes 4227072 | tf_op jit(solution)/shard_map/all_gather | solution.py:23
  78.4 232.6 %reduce-scatter.2.cloned.1.call-start = ((), (), s32[]{:S(2)}) async-start(), calls=%async_computation.4 | async-start | bytes 327680 | tf_op jit(solution)/shard_map/reduce_scatter | solution.py:26
Sparse Core Ops, SparseCore 0:
  81.7 196.5 all-gather.1
  282.9 28.1 reduce-scatter.1
where the time goes:
time: 509 us; the launch traced here: 508 us
  waiting for transfers between devices  386 us (76%)
  other arithmetic  41.6 us (8%)
  starting transfers between devices  27.5 us (5%)
  matrix products  20.2 us (4%)
  local copies, waits for them, and re-layouts  18.5 us (4%)
  between operations  14.1 us (3%)
    all_gather x1, waiting for transfers between devices, body(): lax.all_gather(kv_weight, 'pool', axis=1, tiled=True)  198 us
    all_to_all x1, waiting for transfers between devices, body(): lax.all_to_all(reply, 'pool', split_axis=0, concat_axis=0, tiled=True)  144 us
    reduce_scatter x1, waiting for transfers between devices, body(): lax.psum_scatter(partial_kv.astype(jnp.bfloat16), 'tp', scatter_dimension...  28.2 us
    all_to_all x1, starting transfers between devices, body(): lax.all_to_all(request.reshape(npool, 1), 'pool', split_axis=0, concat_ax...  19.8 us
    eq x1, other arithmetic, body(): incoming == slot + 1  18.3 us
    all_to_all x1, waiting for transfers between devices, body(): lax.all_to_all(request.reshape(npool, 1), 'pool', split_axis=0, concat_ax...  14.4 us
  transfers between devices with their start and end apart: 4, of which 4 were waited for; matrix products, arithmetic and copies ran while one was open for 2% of the time, Pallas kernels for 0%

commit v1 on v0

--- a/solution.py
+++ b/solution.py
@@ -20,7 +20,9 @@
 def body(hidden_rows, kv_weight, queries, cache_table, retrieval, pattern):
     partial_kv = jnp.dot(
         hidden_rows,
-        lax.all_gather(kv_weight, "pool", axis=1, tiled=True),
+        jnp.concatenate(
+            lax.all_to_all(jnp.stack([kv_weight] * lax.axis_size("pool")), "pool", 0, 0), axis=1
+        ),
         preferred_element_type=jnp.float32,
     )
     fresh = lax.psum_scatter(partial_kv.astype(jnp.bfloat16), "tp", scatter_dimension=1, tiled=True)

time: 509 us -> 670 us (1.32)
  waiting for transfers between devices: 386 us -> 519 us
  blocking collectives: 0 us -> 35.1 us
  starting transfers between devices: 27.5 us -> 18.6 us
    all_gather x1 -> x0, waiting for transfers between devices: 198 us -> none  [body(): lax.all_gather(kv_weight, 'pool', axis=1, tiled=True)]
    all_to_all x1, waiting for transfers between devices: 144 us -> 331 us  [body(): lax.all_to_all(reply, 'pool', split_axis=0, concat_axis=0, tiled=True)]
    all_to_all x1, waiting for transfers between devices: 14.4 us -> 161 us  [body(): lax.all_to_all(jnp.stack([kv_weight] * lax.axis_size('pool')), 'pool', 0, 0)]
    all_to_all x0 -> x1, blocking collectives: none -> 35.1 us  [body(): lax.all_to_all(request.reshape(npool, 1), 'pool', split_axis=0, concat_ax...]
    all_to_all x1, starting transfers between devices: 19.8 us -> 7.69 us  [body(): lax.all_to_all(jnp.stack([kv_weight] * lax.axis_size('pool')), 'pool', 0, 0)]
  transfers between devices with their start and end apart: 4 -> 3, of which waited for: 4 -> 3; matrix products, arithmetic and copies ran while one was open for 2% -> 5% of each run, Pallas kernels for 0% -> 0%
where the time goes in v1:
time: 670 us; the launch traced here: 669 us
  waiting for transfers between devices  519 us (77%)
  other arithmetic  41.7 us (6%)
  blocking collectives  35.1 us (5%)
  matrix products  20.2 us (3%)
  local copies, waits for them, and re-layouts  20 us (3%)
  starting transfers between devices  18.6 us (3%)
  between operations  14.2 us (2%)
    all_to_all x1, waiting for transfers between devices, body(): lax.all_to_all(reply, 'pool', split_axis=0, concat_axis=0, tiled=True)  331 us
    all_to_all x1, waiting for transfers between devices, body(): lax.all_to_all(jnp.stack([kv_weight] * lax.axis_size('pool')), 'pool', 0, 0)  161 us
    all_to_all x1, blocking collectives, body(): lax.all_to_all(request.reshape(npool, 1), 'pool', split_axis=0, concat_ax...  35.1 us
    reduce_scatter x1, waiting for transfers between devices, body(): lax.psum_scatter(partial_kv.astype(jnp.bfloat16), 'tp', scatter_dimension...  27.6 us
    eq x1, other arithmetic, body(): incoming == slot + 1  18.4 us
  transfers between devices with their start and end apart: 3, of which 3 were waited for; matrix products, arithmetic and copies ran while one was open for 5% of the time, Pallas kernels for 0%

profile of v1, /device:TPU:24, one launch (start us, length us, event | category | flops | bytes accessed | tf_op | source)
XLA Modules:
  0.0 669.4 jit_solution(5710430382484247807)
XLA Ops:
  8.1 35.1 %all_to_all.19 = s32[128,1,1]{2,1,0:T(1,128)S(1)} all-to-all(s32[128,1,1]{2,1,0:T(1,128)S(1)} %copy.23), channel_id=1, replica_groups=mesh['pool'=128,'tp'=4] {'pool'}, dimensions={0} | all-to-all | bytes 1024 | tf_op jit(solution)/shard_map/all_to_all | solution.py:36
  43.2 3.2 stack.2
  46.4 7.7 %all-to-all-start = ((bf16[128,2048,8]{1,2,0:T(8,128)(2,1)}), bf16[128,2048,8]{1,2,0:T(8,128)(2,1)}, u32[]{:S(2)}, u32[]{:S(2)}) async-start(bf16[128,2048,8]{1,2,0:T(8,128)(2,1)} %stack.2), calls=%async_computation | async-start | bytes 8388608 | tf_op jit(solution)/shard_map/all_to_all | solution.py:24
  54.2 18.4 %compare_reduce_fusion.7 = (pred[128]{0:T(512)(128)(4,1)S(1)}, pred[128]{0:T(512)(128)(4,1)S(1)}, pred[128]{0:T(512)(128)(4,1)S(1)}, pred[128]{0:T(512)(128)(4,1...) fusion(s32[128,1,1]{2,1,0:T(1,128)S(1)} %all_to_all.19), kind=kLoop, calls=%fused_computation.44 | loop fusion | flops 1024 | bytes 1536 | tf_op jit(solution)/shard_map/eq | solution.py:41
  72.6 7.8 %select_select_fusion = bf16[128,128,256]{2,1,0:T(8,128)(2,1)} fusion(pred[128]{0:T(512)(128)(4,1)S(1)} %get-tuple-element.107, pred[128]{0:T(512)(128)(4,1)S(1)} %get-tuple-element.108, pred[128]{0:T(512)(128)(4,1)S(1)} %get-tuple-element.109, pred[128]{0:T(512)(128)(4,1)S(1)} %get-tuple-element.110, pred[128]{0:T(512)(128)(4,1)S(1)} %get-tuple-element.111, ...), kind=kLoop, calls=%fused_computation.20 | loop fusion | flops 33554432 | bytes 8913920 | tf_op jit(solution)/shard_map/jit(_where)/select_n | solution.py:41
  80.4 160.6 %all-to-all-done = bf16[128,2048,8]{1,2,0:T(8,128)(2,1)} async-done(((bf16[128,2048,8]{1,2,0:T(8,128)(2,1)}), bf16[128,2048,8]{1,2,0:T(8,128)(2,1)}, u32[]{:S(2)}, u32[]{:S(2)}) %all-to-all-start) | async-done | bytes 4194336 | tf_op jit(solution)/shard_map/all_to_all | solution.py:24
  241.0 10.8 %all-to-all-start.2 = ((bf16[128,128,256]{2,1,0:T(8,128)(2,1)}), bf16[128,128,256]{2,1,0:T(8,128)(2,1)}, u32[]{:S(2)}, u32[]{:S(2)}) async-start(bf16[128,128,256]{2,1,0:T(8,128)(2,1)} %select_select_fusion), calls=%async_computation.3 | async-start | bytes 16777216 | tf_op jit(solution)/shard_map/all_to_all | solution.py:42
  253.5 4.4 fusion.12
  258.0 27.6 %reduce-scatter.2.cloned.1.call-done = bf16[128,256]{1,0:T(8,128)(2,1)} async-done(((bf16[128,1024]{1,0:T(8,128)(2,1)}), bf16[128,256]{1,0:T(8,128)(2,1)}) %reduce-scatter.2.cloned.1.call-update) | async-done | bytes 65552 | tf_op jit(solution)/shard_map/reduce_scatter | solution.py:28
  285.7 1.0 select_reduce_fusion
  286.8 1.0 fusion.17
  287.9 330.8 %all-to-all-done.2 = bf16[128,128,256]{2,1,0:T(8,128)(2,1)} async-done(((bf16[128,128,256]{2,1,0:T(8,128)(2,1)}), bf16[128,128,256]{2,1,0:T(8,128)(2,1)}, u32[]{:S(2)}, u32[]{:S(2)}) %all-to-all-start.2) | async-done | bytes 8388640 | tf_op jit(solution)/shard_map/all_to_all | solution.py:42
  618.6 6.2 gather_fusion
  624.8 5.3 bitcast_select_fusion.2
  630.1 31.4 %while.15 = (s32[]{:T(128)}, f32[1024]{0:T(1024)S(1)}, f32[1024]{0:T(1024)S(1)}, f32[1024,128]{1,0:T(8,128)S(1)}, s32[8,2,8]{2,0,1:T(8,128)S(1)}, /*index=5*/bf1...) while((s32[]{:T(128)}, f32[1024]{0:T(1024)S(1)}, ...), condition=%wide.region_8.9_spmd.clone, body=%wide.region_4.8_spmd.clone.sunk | while | flops 545550336 | bytes 15561029 | solution.py:87
  630.2 1.1 dynamic-slice_bitcast_fusion.2
  633.0 1.0 convolution_add_fusion.2
  634.1 1.1 dynamic-slice_bitcast_fusion.2
  638.1 1.1 dynamic-slice_bitcast_fusion.2
  642.0 1.1 dynamic-slice_bitcast_fusion.2
  645.9 1.1 dynamic-slice_bitcast_fusion.2
  649.8 1.1 dynamic-slice_bitcast_fusion.2
  653.8 1.1 dynamic-slice_bitcast_fusion.2
  657.7 1.1 dynamic-slice_bitcast_fusion.2
  (110 shorter events, 25.1 us)
Async XLA Ops:
  7.2 246.3 %copy-start = (bf16[128,2048]{1,0:T(8,128)(2,1)S(1)}, bf16[128,2048]{1,0:T(8,128)(2,1)}, u32[]{:S(2)}) copy-start(bf16[128,2048]{1,0:T(8,128)(2,1)} %param.8) | copy-start | bytes 1572868
  46.4 7.7 %copy-start.1 = (bf16[8,128,256]{2,1,0:T(8,128)(2,1)S(1)}, bf16[8,128,256]{2,1,0:T(8,128)(2,1)}, u32[]{:S(2)}) copy-start(bf16[8,128,256]{2,1,0:T(8,128)(2,1)} %param.11) | copy-start | bytes 1572868
  46.4 194.5 %all-to-all-start = ((bf16[128,2048,8]{1,2,0:T(8,128)(2,1)}), bf16[128,2048,8]{1,2,0:T(8,128)(2,1)}, u32[]{:S(2)}, u32[]{:S(2)}) async-start(bf16[128,2048,8]{1,2,0:T(8,128)(2,1)} %stack.2), calls=%async_computation | async-start | bytes 8388608 | tf_op jit(solution)/shard_map/all_to_all | solution.py:24
  80.4 172.0 %copy-start.4 = (s32[1,64]{1,0:T(1,128)S(1)}, s32[1,64]{1,0:T(1,128)}, u32[]{:S(2)}) copy-start(s32[1,64]{1,0:T(1,128)} %param.12) | copy-start | bytes 772
  80.4 172.9 %copy-start.2 = (bf16[128,1024]{1,0:T(8,128)(2,1)S(1)}, bf16[128,1024]{1,0:T(8,128)(2,1)}, u32[]{:S(2)}) copy-start(bf16[128,1024]{1,0:T(8,128)(2,1)} %param.10) | copy-start | bytes 786436
  80.4 173.0 %copy-start.3 = (s32[1,2,64]{2,1,0:T(2,128)S(1)}, s32[1,2,64]{2,1,0:T(2,128)}, u32[]{:S(2)}) copy-start(s32[1,2,64]{2,1,0:T(2,128)} %param.13) | copy-start | bytes 1540
  241.0 377.7 %all-to-all-start.2 = ((bf16[128,128,256]{2,1,0:T(8,128)(2,1)}), bf16[128,128,256]{2,1,0:T(8,128)(2,1)}, u32[]{:S(2)}, u32[]{:S(2)}) async-start(bf16[128,128,256]{2,1,0:T(8,128)(2,1)} %select_select_fusion), calls=%async_computation.3 | async-start | bytes 16777216 | tf_op jit(solution)/shard_map/all_to_all | solution.py:42
  251.8 33.8 %reduce-scatter.2.cloned.1.call-start = ((), (), s32[]{:S(2)}) async-start(), calls=%async_computation.4 | async-start | bytes 327680 | tf_op jit(solution)/shard_map/reduce_scatter | solution.py:28
Sparse Core Ops, SparseCore 0:
  258.0 27.5 reduce-scatter.1
